TPU v7x, 32 devices: a whole 2x2x4 slice. The times are simulated.
32 devices in a mesh: tile: 8 (over y, x, core), slab: 4 (over z).
Axes of the slice: x: 2, y: 2, z: 4, core: 2. Of those that a mesh axis runs over, the one named last changes fastest.
Arguments:
- estimate: float32 [64, 128, 512], P('slab', 'tile'), may hold values from 0.5 to 2
- observed: float32 [64, 128, 512], P('slab', 'tile'), may hold values from 0.25 to 4
- kernel_rows: float32 [31], replicated, may hold values from 0.001 to 1
- kernel_columns: float32 [31], replicated, may hold values from 0.001 to 1
- kernel_planes: float32 [31], replicated, may hold values from 0.001 to 1
Outputs:
- new_estimate: float32 [64, 128, 512], P('slab', 'tile')
- pyramid_level: float32 [64, 64, 256], P('slab', 'tile')
All inputs are finite; a program needn't handle non-finite values.
Results may differ from a plain program's by a relative error of at most 0.00005.
Values sent between devices are 32-bit elements; how exact they have to be, the bound alone decides.
No kernel may reach another device: no remote copies, remote signals or barrier semaphores. Data moves between devices by JAX's collectives and lax.ppermute only.
A program may use at most 64 MiB of HBM per device.

v0:
```python
import jax
import jax.numpy as jnp
from jax import lax
from jax.sharding import PartitionSpec as P

PRECISE = lax.Precision.HIGHEST


def extended(shard, sides, width):
    for axis, dim in sides:
        devices, length = (lax.axis_size(axis), shard.shape[dim])
        up = [(i, (i + 1) % devices) for i in range(devices - 1)]
        down = [(j, i) for i, j in up]
        last = lax.slice_in_dim(shard, length - width, length, axis=dim)
        initial = lax.slice_in_dim(shard, 0, width, axis=dim)
        before = lax.ppermute(last, axis, up)
        after = lax.ppermute(initial, axis, down)
        shard = jnp.concatenate([before, shard, after], axis=dim)
    return shard


def banded(kernel, row_count, col_count, orient, anchor):
    tap_count = kernel.shape[0]
    offset_index = (
        orient
        * (
            lax.broadcasted_iota(jnp.int32, (row_count, col_count), 0)
            - lax.broadcasted_iota(jnp.int32, (row_count, col_count), 1)
        )
        + anchor
    )
    inside = (offset_index >= 0) & (offset_index < tap_count)
    values = jnp.take(kernel, jnp.clip(offset_index, 0, tap_count - 1))
    return jnp.where(inside, values, jnp.zeros_like(values))


def pyramid_matrix(row_count, col_count, anchor):
    offset_index = (
        lax.broadcasted_iota(jnp.int32, (row_count, col_count), 0)
        - 2 * lax.broadcasted_iota(jnp.int32, (row_count, col_count), 1)
        + anchor
    )
    outer = (offset_index == 0) | (offset_index == 3)
    middle = (offset_index == 1) | (offset_index == 2)
    return jnp.where(
        outer, jnp.float32(0.125), jnp.where(middle, jnp.float32(0.375), jnp.float32(0.0))
    )


def across_depth(volume, matrix):
    return jnp.einsum("pxy,pq->qxy", volume, matrix, precision=PRECISE)


def across_rows(volume, matrix):
    return jnp.einsum("zpy,pq->zqy", volume, matrix, precision=PRECISE)


def across_columns(volume, matrix):
    return jnp.dot(volume, matrix, precision=PRECISE)


def shards(estimate, observed, kernel_rows, kernel_columns, kernel_planes):
    plane_count, row_count, col_count = estimate.shape
    reach_cells = (kernel_rows.shape[0] - 1) // 2
    groups = lax.axis_size("slab")
    planes_all = plane_count * groups
    padded = extended(estimate, (("tile", 1),), reach_cells)
    partial_value = across_rows(
        padded, banded(kernel_rows, row_count + 2 * reach_cells, row_count, 1, 0)
    )
    partial_value = across_columns(
        partial_value, banded(kernel_columns, col_count, col_count, 1, reach_cells)
    )
    forward_depth = banded(kernel_planes, planes_all, planes_all, 1, reach_cells)
    backward_depth = banded(kernel_planes, planes_all, planes_all, -1, reach_cells)
    turned = across_depth(
        lax.all_to_all(partial_value, "slab", split_axis=2, concat_axis=0, tiled=True),
        forward_depth,
    )
    blurred = lax.all_to_all(turned, "slab", split_axis=0, concat_axis=2, tiled=True)
    quotient = observed / blurred
    turned_back = across_depth(
        lax.all_to_all(quotient, "slab", split_axis=2, concat_axis=0, tiled=True), backward_depth
    )
    back_field = lax.all_to_all(turned_back, "slab", split_axis=0, concat_axis=2, tiled=True)
    spread = across_columns(
        back_field, banded(kernel_columns, col_count, col_count, -1, reach_cells)
    )
    padded_spread = extended(spread, (("tile", 1),), reach_cells)
    correction = across_rows(
        padded_spread,
        banded(kernel_rows, row_count + 2 * reach_cells, row_count, -1, 2 * reach_cells),
    )
    new_estimate = estimate * correction
    halved = across_columns(new_estimate, pyramid_matrix(col_count, col_count // 2, 1))
    padded_halved = extended(halved, (("tile", 1),), 1)
    pyramid_level = across_rows(padded_halved, pyramid_matrix(row_count + 2, row_count // 2, 0))
    return (new_estimate, pyramid_level)


def solution(mesh):
    in_specs = (P("slab", "tile", None), P("slab", "tile", None), P(), P(), P())
    out_specs = (P("slab", "tile", None), P("slab", "tile", None))
    return jax.shard_map(shards, mesh=mesh, in_specs=in_specs, out_specs=out_specs, check_vma=False)
```

profile of v0, /device:TPU:1, one launch (start us, length us, event | category | flops | bytes accessed | tf_op | source)
XLA Modules:
  0.0 230.6 jit_solution(3255726964246776414)
XLA Ops:
  2.0 4.5 %collective-permute-start = (f32[16,15,512]{2,1,0:T(8,128)S(1)}, f32[16,15,512]{2,1,0:T(8,128)S(1)}, u32[]{:S(2)}, u32[]{:S(2)}) collective-permute-start(f32[16,15,512]{2,1,0:T(8,128)S(1)} %get-tuple-element.7), channel_id=1, source_target_pairs={{0,4},{4,8},{8,12},{12,16},{16,20},{20,24},{24,28},{1,5},{5,9},{9,... | collective-permute-start | bytes 1474568 | tf_op jit(solution)/shard_map/ppermute | solution.py:16
  8.6 4.8 %gather_fusion.3 = f32[736]{0:T(1024)S(1)} fusion(f32[31]{0:T(128)S(1)} %copy-done.1, s32[1024]{0:T(1024)S(1)} %pad_clamp_fusion), kind=kCustom, calls=%fused_computation.2.clone | custom fusion | bytes 8832 | tf_op jit(solution)/shard_map/jit(_take)/gather | solution.py:33
  14.9 5.0 %collective-permute-done.1 = f32[16,15,512]{2,1,0:T(8,128)S(1)} collective-permute-done((f32[16,15,512]{2,1,0:T(8,128)S(1)}, f32[16,15,512]{2,1,0:T(8,128)S(1)}, u32[]{:S(2)}, u32[]{:S(2)}) %collective-permute-start.1) | collective-permute-done | bytes 491552 | tf_op jit(solution)/shard_map/ppermute | solution.py:17
  20.9 23.0 %fusion.23 = f32[16,16,512]{2,1,0:T(8,128)S(1)} fusion(f32[16,16,512]{2,1,0:T(8,128)S(1)} %fusion.15, f32[]{:T(128)} %bitcast.35, f32[]{:T(128)} %bitcast.34, f32[]{:T(128)} %bitcast.33, f32[]{:T(128)} %bitcast.32, f32[]{:T(128)} %bitcast.31, f32[]{:T(128)} %bitcast.30, f32[]{:T(128)} %bitcast.29, f32[]{:T(128)} %bitcast.28, f32[]{:T(128)} %bitcast.27, ...), kind=kOutput, calls=%fused_computation.25 | convolution fusion | flops 824705024 | bytes 1048700 | tf_op jit(solution)/shard_map/dot_general | solution.py:59
  43.9 3.6 %copy.19 = f32[16,16,512]{1,0,2:T(8,128)} copy(f32[16,16,512]{2,1,0:T(8,128)S(1)} %fusion.23) | data formatting | bytes 1048576 | tf_op jit(solution)/shard_map/dot_general | solution.py:59
  47.5 4.6 %reshape.229 = f32[4,1,32768]{2,1,0:T(1,128)} reshape(f32[512,16,16]{2,1,0:T(8,128)} %bitcast.121) | data formatting | bytes 1048576
  52.1 4.6 %all-to-all-start = ((f32[4,1,32768]{2,1,0:T(1,128)}), f32[4,1,32768]{2,1,0:T(1,128)S(1)}, u32[]{:S(2)}, u32[]{:S(2)}) async-start(f32[4,1,32768]{2,1,0:T(1,128)} %reshape.229), calls=%async_computation | async-start | bytes 1048576 | tf_op jit(solution)/shard_map/all_to_all | solution.py:77
  56.8 24.7 %gather_fusion.2 = f32[4096]{0:T(1024)S(1)} fusion(f32[31]{0:T(128)S(1)} %copy-done, s32[4096]{0:T(1024)S(1)} %broadcast_clamp_fusion), kind=kCustom, calls=%fused_computation.3.clone | custom fusion | bytes 49152 | tf_op jit(solution)/shard_map/jit(_take)/gather | solution.py:33
  84.2 3.4 %reshape.230 = f32[512,16,16]{2,1,0:T(8,128)} reshape(f32[4,32768]{1,0:T(4,128)S(1)} %reduce) | data formatting | bytes 1048576
  87.7 3.3 %copy.20 = f32[16,16,4,128]{3,0,2,1:T(8,128)S(1)} copy(f32[16,16,4,128]{1,0,3,2:T(8,128)} %bitcast.122) | data formatting | bytes 1048576 | tf_op jit(solution)/shard_map/all_to_all | solution.py:77
  92.8 4.5 %all-to-all-start.1 = ((f32[64,16,128]{2,1,0:T(8,128)}), f32[64,16,128]{2,1,0:T(8,128)S(1)}, u32[]{:S(2)}, u32[]{:S(2)}) async-start(f32[64,16,128]{2,1,0:T(8,128)} %copy.22), calls=%async_computation.1 | async-start | bytes 1048576 | tf_op jit(solution)/shard_map/all_to_all | solution.py:80
  97.3 3.7 %copy.24 = f32[16,16,512]{1,0,2:T(8,128)} copy(f32[16,16,512]{2,1,0:T(8,128)S(1)} %copy-done.3) | data formatting | bytes 1048576 | tf_op args[1]
  100.9 5.6 %all-to-all-done.1 = f32[64,16,128]{2,1,0:T(8,128)S(1)} async-done(((f32[64,16,128]{2,1,0:T(8,128)}), f32[64,16,128]{2,1,0:T(8,128)S(1)}, u32[]{:S(2)}, u32[]{:S(2)}) %all-to-all-start.1) | async-done | bytes 524320 | tf_op jit(solution)/shard_map/all_to_all | solution.py:80
  109.3 6.0 %bitcast_divide_fusion = f32[16,16,512]{1,0,2:T(8,128)} fusion(f32[16,16,512]{1,0,2:T(8,128)} %copy.24, f32[16,16,4,128]{1,0,3,2:T(8,128)} %copy.23), kind=kLoop, calls=%fused_computation.4 | loop fusion | flops 131072 | bytes 1572864 | tf_op jit(solution)/shard_map/div | solution.py:81
  115.3 4.6 %reshape.231 = f32[4,1,32768]{2,1,0:T(1,128)} reshape(f32[512,16,16]{2,1,0:T(8,128)} %bitcast.120) | data formatting | bytes 1048576
  119.9 3.5 %all-to-all-start.2 = ((f32[4,1,32768]{2,1,0:T(1,128)}), f32[4,1,32768]{2,1,0:T(1,128)S(1)}, u32[]{:S(2)}, u32[]{:S(2)}) async-start(f32[4,1,32768]{2,1,0:T(1,128)} %reshape.231), calls=%async_computation.2 | async-start | bytes 1048576 | tf_op jit(solution)/shard_map/all_to_all | solution.py:83
  123.5 24.7 %gather_fusion.1 = f32[4096]{0:T(1024)S(1)} fusion(f32[31]{0:T(128)S(1)} %copy-done, s32[4096]{0:T(1024)S(1)} %broadcast_clamp_fusion.1), kind=kCustom, calls=%fused_computation.1.clone | custom fusion | bytes 49152 | tf_op jit(solution)/shard_map/jit(_take)/gather | solution.py:33
  150.4 3.4 %reshape.232 = f32[512,16,16]{2,1,0:T(8,128)} reshape(f32[4,32768]{1,0:T(4,128)S(1)} %reduce.1) | data formatting | bytes 1048576
  153.8 3.3 %copy.25 = f32[16,16,4,128]{3,0,2,1:T(8,128)S(1)} copy(f32[16,16,4,128]{1,0,3,2:T(8,128)} %bitcast.123) | data formatting | bytes 1048576 | tf_op jit(solution)/shard_map/all_to_all | solution.py:83
  158.1 15.2 %all_to_all.72 = f32[64,16,128]{2,1,0:T(8,128)S(1)} all-to-all(f32[64,16,128]{2,1,0:T(8,128)S(1)} %copy.27), channel_id=1, replica_groups=mesh['tile'=8,'slab'=4] {'slab'}, dimensions={0} | all-to-all | bytes 1048576 | tf_op jit(solution)/shard_map/all_to_all | solution.py:85
  174.0 22.9 %fusion.21 = f32[16,16,512]{2,1,0:T(8,128)S(1)} fusion(f32[16,16,512]{2,1,0:T(8,128)S(1)} %all_to_all.67, f32[]{:T(128)} %bitcast.35, f32[]{:T(128)} %bitcast.34, f32[]{:T(128)} %bitcast.33, f32[]{:T(128)} %bitcast.32, f32[]{:T(128)} %bitcast.31, f32[]{:T(128)} %bitcast.30, f32[]{:T(128)} %bitcast.29, f32[]{:T(128)} %bitcast.28, f32[]{:T(128)} %bitcast.27, ...), kind=kOutput, calls=%fused_computation.23 | convolution fusion | flops 824967168 | bytes 1048700 | tf_op jit(solution)/shard_map/dot_general | solution.py:59
  197.0 13.3 %collective-permute-start.2 = (f32[16,15,512]{2,1,0:T(8,128)S(1)}, f32[16,15,512]{2,1,0:T(8,128)S(1)}, u32[]{:S(2)}, u32[]{:S(2)}) collective-permute-start(f32[16,15,512]{2,1,0:T(8,128)S(1)} %get-tuple-element.4), channel_id=1, source_target_pairs={{0,4},{4,8},{8,12},{12,16},{16,20},{20,24},{24,28},{1,5},{5,9},{9,... | collective-permute-start | bytes 1474568 | tf_op jit(solution)/shard_map/ppermute | solution.py:16
  212.5 4.8 %gather_fusion = f32[736]{0:T(1024)S(1)} fusion(f32[31]{0:T(128)S(1)} %copy-done.1, s32[1024]{0:T(1024)S(1)} %pad_clamp_fusion.1), kind=kCustom, calls=%fused_computation.clone | custom fusion | bytes 8832 | tf_op jit(solution)/shard_map/jit(_take)/gather | solution.py:33
  217.4 3.4 %collective-permute-done.3 = f32[16,15,512]{2,1,0:T(8,128)S(1)} collective-permute-done((f32[16,15,512]{2,1,0:T(8,128)S(1)}, f32[16,15,512]{2,1,0:T(8,128)S(1)}, u32[]{:S(2)}, u32[]{:S(2)}) %collective-permute-start.3) | collective-permute-done | bytes 491552 | tf_op jit(solution)/shard_map/ppermute | solution.py:17
  (59 shorter events, 29.2 us)
Async XLA Ops:
  0.6 56.2 %copy-start = (f32[31]{0:T(128)S(1)}, f32[31]{0:T(128)}, u32[]{:S(2)}) copy-start(f32[31]{0:T(128)} %param.15) | copy-start | bytes 376
  0.6 7.9 %copy-start.1 = (f32[31]{0:T(128)S(1)}, f32[31]{0:T(128)}, u32[]{:S(2)}) copy-start(f32[31]{0:T(128)} %param.13) | copy-start | bytes 376
  2.0 12.9 %collective-permute-start = (f32[16,15,512]{2,1,0:T(8,128)S(1)}, f32[16,15,512]{2,1,0:T(8,128)S(1)}, u32[]{:S(2)}, u32[]{:S(2)}) collective-permute-start(f32[16,15,512]{2,1,0:T(8,128)S(1)} %get-tuple-element.7), channel_id=1, source_target_pairs={{0,4},{4,8},{8,12},{12,16},{16,20},{20,24},{24,28},{1,5},{5,9},{9,... | collective-permute-start | bytes 1474568 | tf_op jit(solution)/shard_map/ppermute | solution.py:16
  6.5 13.4 %collective-permute-start.1 = (f32[16,15,512]{2,1,0:T(8,128)S(1)}, f32[16,15,512]{2,1,0:T(8,128)S(1)}, u32[]{:S(2)}, u32[]{:S(2)}) collective-permute-start(f32[16,15,512]{2,1,0:T(8,128)S(1)} %get-tuple-element.8), channel_id=1, source_target_pairs={{4,0},{8,4},{12,8},{16,12},{20,16},{24,20},{28,24},{5,1},{9,5},{13... | collective-permute-start | bytes 1474568 | tf_op jit(solution)/shard_map/ppermute | solution.py:17
  8.6 4.9 %copy-start.5 = (f32[31]{0:T(128)S(1)}, f32[31]{0:T(128)}, u32[]{:S(2)}) copy-start(f32[31]{0:T(128)} %param.14) | copy-start | bytes 376
  8.6 11.3 %copy-start.2 = (f32[16,16,512]{2,1,0:T(8,128)S(1)}, f32[16,16,512]{2,1,0:T(8,128)}, u32[]{:S(2)}) copy-start(f32[16,16,512]{2,1,0:T(8,128)} %param.11) | copy-start | bytes 1572868
  52.1 29.5 %all-to-all-start = ((f32[4,1,32768]{2,1,0:T(1,128)}), f32[4,1,32768]{2,1,0:T(1,128)S(1)}, u32[]{:S(2)}, u32[]{:S(2)}) async-start(f32[4,1,32768]{2,1,0:T(1,128)} %reshape.229), calls=%async_computation | async-start | bytes 1048576 | tf_op jit(solution)/shard_map/all_to_all | solution.py:77
  91.0 6.3 %copy-start.3 = (f32[16,16,512]{2,1,0:T(8,128)S(1)}, f32[16,16,512]{2,1,0:T(8,128)}, u32[]{:S(2)}) copy-start(f32[16,16,512]{2,1,0:T(8,128)} %param.12) | copy-start | bytes 1572868
  92.8 13.7 %all-to-all-start.1 = ((f32[64,16,128]{2,1,0:T(8,128)}), f32[64,16,128]{2,1,0:T(8,128)S(1)}, u32[]{:S(2)}, u32[]{:S(2)}) async-start(f32[64,16,128]{2,1,0:T(8,128)} %copy.22), calls=%async_computation.1 | async-start | bytes 1048576 | tf_op jit(solution)/shard_map/all_to_all | solution.py:80
  119.9 28.4 %all-to-all-start.2 = ((f32[4,1,32768]{2,1,0:T(1,128)}), f32[4,1,32768]{2,1,0:T(1,128)S(1)}, u32[]{:S(2)}, u32[]{:S(2)}) async-start(f32[4,1,32768]{2,1,0:T(1,128)} %reshape.231), calls=%async_computation.2 | async-start | bytes 1048576 | tf_op jit(solution)/shard_map/all_to_all | solution.py:83
  197.0 20.4 %collective-permute-start.2 = (f32[16,15,512]{2,1,0:T(8,128)S(1)}, f32[16,15,512]{2,1,0:T(8,128)S(1)}, u32[]{:S(2)}, u32[]{:S(2)}) collective-permute-start(f32[16,15,512]{2,1,0:T(8,128)S(1)} %get-tuple-element.4), channel_id=1, source_target_pairs={{0,4},{4,8},{8,12},{12,16},{16,20},{20,24},{24,28},{1,5},{5,9},{9,... | collective-permute-start | bytes 1474568 | tf_op jit(solution)/shard_map/ppermute | solution.py:16
  210.3 10.5 %collective-permute-start.3 = (f32[16,15,512]{2,1,0:T(8,128)S(1)}, f32[16,15,512]{2,1,0:T(8,128)S(1)}, u32[]{:S(2)}, u32[]{:S(2)}) collective-permute-start(f32[16,15,512]{2,1,0:T(8,128)S(1)} %get-tuple-element.6), channel_id=1, source_target_pairs={{4,0},{8,4},{12,8},{16,12},{20,16},{24,20},{28,24},{5,1},{9,5},{13... | collective-permute-start | bytes 1474568 | tf_op jit(solution)/shard_map/ppermute | solution.py:17
  221.8 8.8 %copy-start.4 = (f32[16,16,512]{2,1,0:T(8,128)}, f32[16,16,512]{2,1,0:T(8,128)S(1)}, u32[]{:S(2)}) copy-start(f32[16,16,512]{2,1,0:T(8,128)S(1)} %fusion.18) | copy-start | bytes 1572868
  222.6 4.4 %collective-permute-start.4 = (f32[16,1,256]{2,1,0:T(1,128)S(1)}, f32[16,1,256]{2,1,0:T(1,128)S(1)}, u32[]{:S(2)}, u32[]{:S(2)}) collective-permute-start(f32[16,1,256]{2,1,0:T(1,128)S(1)} %get-tuple-element.9), channel_id=1, source_target_pairs={{0,4},{4,8},{8,12},{12,16},{16,20},{20,24},{24,28},{1,5},{5,9},{9,... | collective-permute-start | bytes 49160 | tf_op jit(solution)/shard_map/ppermute | solution.py:16
  224.5 5.1 %collective-permute-start.5 = (f32[16,1,256]{2,1,0:T(1,128)S(1)}, f32[16,1,256]{2,1,0:T(1,128)S(1)}, u32[]{:S(2)}, u32[]{:S(2)}) collective-permute-start(f32[16,1,256]{2,1,0:T(1,128)S(1)} %get-tuple-element.10), channel_id=1, source_target_pairs={{4,0},{8,4},{12,8},{16,12},{20,16},{24,20},{28,24},{5,1},{9,5},{13... | collective-permute-start | bytes 49160 | tf_op jit(solution)/shard_map/ppermute | solution.py:17
where the time goes:
time: 232 us; the launch traced here: 231 us
  local copies, waits for them, and re-layouts  97.8 us (42%)
  matrix products  50.9 us (22%)
  starting transfers between devices  38.8 us (17%)
  waiting for transfers between devices  16.6 us (7%)
  blocking collectives  15.2 us (7%)
  other arithmetic  10.3 us (4%)
    gather x10, local copies, waits for them, and re-layouts, banded(): values = jnp.take(kernel, jnp.clip(offset_index, 0, tap_count - 1))  60.7 us
    dot_general x3, matrix products, across_columns(): return jnp.dot(volume, matrix, precision=PRECISE)  46.6 us
    unnamed x17, local copies, waits for them, and re-layouts  19.8 us
    ppermute x3, starting transfers between devices, extended(): before = lax.ppermute(last, axis, up)  19.7 us
    all_to_all x1, blocking collectives, shards(): lax.all_to_all(turned_back, 'slab', split_axis=0, concat_axis=2, tiled=True)  15.2 us
    ppermute x3, waiting for transfers between devices, extended(): after = lax.ppermute(initial, axis, down)  11 us
    ppermute x3, starting transfers between devices, extended(): after = lax.ppermute(initial, axis, down)  6.46 us
    div x1, other arithmetic, shards(): quotient = observed / blurred  5.99 us
  transfers between devices with their start and end apart: 9, of which 4 were waited for; matrix products, arithmetic and copies ran while one was open for 28% of the time, Pallas kernels for 0%

commit v1 on v0

--- a/solution.py
+++ b/solution.py
@@ -82,7 +82,16 @@
     turned_back = across_depth(
         lax.all_to_all(quotient, "slab", split_axis=2, concat_axis=0, tiled=True), backward_depth
     )
-    back_field = lax.all_to_all(turned_back, "slab", split_axis=0, concat_axis=2, tiled=True)
+
+    def hubs_lift(incoming_x):
+        f_now = lax.axis_size("slab")
+        block_out = jnp.split(incoming_x, f_now, 0)
+        earlier = jnp.stack(block_out)
+        work_now = lax.all_to_all(earlier, "slab", 0, 0)
+        piece_out = jnp.concatenate(work_now, 2)
+        return piece_out
+
+    back_field = hubs_lift(turned_back)
     spread = across_columns(
         back_field, banded(kernel_columns, col_count, col_count, -1, reach_cells)
     )

time: 232 us -> 232 us (level)
  no operation moved by 1% of the time
where the time goes in v1:
time: 232 us; the launch traced here: 230 us
  local copies, waits for them, and re-layouts  97.6 us (42%)
  matrix products  50.8 us (22%)
  starting transfers between devices  38.8 us (17%)
  waiting for transfers between devices  16.5 us (7%)
  blocking collectives  15.2 us (7%)
  other arithmetic  10.4 us (4%)
    gather x10, local copies, waits for them, and re-layouts, banded(): values = jnp.take(kernel, jnp.clip(offset_index, 0, tap_count - 1))  60.7 us
    dot_general x3, matrix products, across_columns(): return jnp.dot(volume, matrix, precision=PRECISE)  46.5 us
    unnamed x17, local copies, waits for them, and re-layouts  19.8 us
    ppermute x3, starting transfers between devices, extended(): before = lax.ppermute(last, axis, up)  19.7 us
    all_to_all x1, blocking collectives, hubs_lift(): work_now = lax.all_to_all(earlier, 'slab', 0, 0)  15.2 us
    ppermute x3, waiting for transfers between devices, extended(): after = lax.ppermute(initial, axis, down)  11 us
    ppermute x3, starting transfers between devices, extended(): after = lax.ppermute(initial, axis, down)  6.46 us
    div x1, other arithmetic, shards(): quotient = observed / blurred  6 us
  transfers between devices with their start and end apart: 9, of which 4 were waited for; matrix products, arithmetic and copies ran while one was open for 28% of the time, Pallas kernels for 0%

profile of v1, /device:TPU:1, one launch (start us, length us, event | category | flops | bytes accessed | tf_op | source)
XLA Modules:
  0.0 230.4 jit_solution(13871363637346014088)
XLA Ops:
  2.0 4.5 %collective-permute-start = (f32[16,15,512]{2,1,0:T(8,128)S(1)}, f32[16,15,512]{2,1,0:T(8,128)S(1)}, u32[]{:S(2)}, u32[]{:S(2)}) collective-permute-start(f32[16,15,512]{2,1,0:T(8,128)S(1)} %get-tuple-element.11), channel_id=1, source_target_pairs={{0,4},{4,8},{8,12},{12,16},{16,20},{20,24},{24,28},{1,5},{5,9},{9,... | collective-permute-start | bytes 1474568 | tf_op jit(solution)/shard_map/ppermute | solution.py:16
  8.6 4.8 %gather_fusion.3 = f32[736]{0:T(1024)S(1)} fusion(f32[31]{0:T(128)S(1)} %copy-done.1, s32[1024]{0:T(1024)S(1)} %pad_clamp_fusion), kind=kCustom, calls=%fused_computation.2.clone | custom fusion | bytes 8832 | tf_op jit(solution)/shard_map/jit(_take)/gather | solution.py:33
  14.9 5.0 %collective-permute-done.1 = f32[16,15,512]{2,1,0:T(8,128)S(1)} collective-permute-done((f32[16,15,512]{2,1,0:T(8,128)S(1)}, f32[16,15,512]{2,1,0:T(8,128)S(1)}, u32[]{:S(2)}, u32[]{:S(2)}) %collective-permute-start.1) | collective-permute-done | bytes 491552 | tf_op jit(solution)/shard_map/ppermute | solution.py:17
  20.9 22.9 %fusion.23 = f32[16,16,512]{2,1,0:T(8,128)S(1)} fusion(f32[16,16,512]{2,1,0:T(8,128)S(1)} %fusion.15, f32[]{:T(128)} %bitcast.35, f32[]{:T(128)} %bitcast.34, f32[]{:T(128)} %bitcast.33, f32[]{:T(128)} %bitcast.32, f32[]{:T(128)} %bitcast.31, f32[]{:T(128)} %bitcast.30, f32[]{:T(128)} %bitcast.29, f32[]{:T(128)} %bitcast.28, f32[]{:T(128)} %bitcast.27, ...), kind=kOutput, calls=%fused_computation.25 | convolution fusion | flops 824705024 | bytes 1048700 | tf_op jit(solution)/shard_map/dot_general | solution.py:59
  43.8 3.6 %copy.18 = f32[16,16,512]{1,0,2:T(8,128)} copy(f32[16,16,512]{2,1,0:T(8,128)S(1)} %fusion.23) | data formatting | bytes 1048576 | tf_op jit(solution)/shard_map/dot_general | solution.py:59
  47.5 4.6 %reshape.237 = f32[4,1,32768]{2,1,0:T(1,128)} reshape(f32[512,16,16]{2,1,0:T(8,128)} %bitcast.126) | data formatting | bytes 1048576
  52.1 4.6 %all-to-all-start = ((f32[4,1,32768]{2,1,0:T(1,128)}), f32[4,1,32768]{2,1,0:T(1,128)S(1)}, u32[]{:S(2)}, u32[]{:S(2)}) async-start(f32[4,1,32768]{2,1,0:T(1,128)} %reshape.237), calls=%async_computation | async-start | bytes 1048576 | tf_op jit(solution)/shard_map/all_to_all | solution.py:77
  56.8 24.7 %gather_fusion.2 = f32[4096]{0:T(1024)S(1)} fusion(f32[31]{0:T(128)S(1)} %copy-done, s32[4096]{0:T(1024)S(1)} %broadcast_clamp_fusion), kind=kCustom, calls=%fused_computation.3.clone | custom fusion | bytes 49152 | tf_op jit(solution)/shard_map/jit(_take)/gather | solution.py:33
  84.2 3.4 %reshape.238 = f32[512,16,16]{2,1,0:T(8,128)} reshape(f32[4,32768]{1,0:T(4,128)S(1)} %reduce) | data formatting | bytes 1048576
  87.7 3.3 %copy.19 = f32[16,16,4,128]{3,0,2,1:T(8,128)S(1)} copy(f32[16,16,4,128]{1,0,3,2:T(8,128)} %bitcast.127) | data formatting | bytes 1048576 | tf_op jit(solution)/shard_map/all_to_all | solution.py:77
  92.8 4.5 %all-to-all-start.1 = ((f32[64,16,128]{2,1,0:T(8,128)}), f32[64,16,128]{2,1,0:T(8,128)S(1)}, u32[]{:S(2)}, u32[]{:S(2)}) async-start(f32[64,16,128]{2,1,0:T(8,128)} %copy.21), calls=%async_computation.1 | async-start | bytes 1048576 | tf_op jit(solution)/shard_map/all_to_all | solution.py:80
  97.3 3.7 %copy.23 = f32[16,16,512]{1,0,2:T(8,128)} copy(f32[16,16,512]{2,1,0:T(8,128)S(1)} %copy-done.3) | data formatting | bytes 1048576 | tf_op args[1]
  101.0 5.5 %all-to-all-done.1 = f32[64,16,128]{2,1,0:T(8,128)S(1)} async-done(((f32[64,16,128]{2,1,0:T(8,128)}), f32[64,16,128]{2,1,0:T(8,128)S(1)}, u32[]{:S(2)}, u32[]{:S(2)}) %all-to-all-start.1) | async-done | bytes 524320 | tf_op jit(solution)/shard_map/all_to_all | solution.py:80
  109.3 6.0 %bitcast_divide_fusion = f32[16,16,512]{1,0,2:T(8,128)} fusion(f32[16,16,512]{1,0,2:T(8,128)} %copy.23, f32[16,16,4,128]{1,0,3,2:T(8,128)} %copy.22), kind=kLoop, calls=%fused_computation.4 | loop fusion | flops 131072 | bytes 1572864 | tf_op jit(solution)/shard_map/div | solution.py:81
  115.3 4.6 %reshape.239 = f32[4,1,32768]{2,1,0:T(1,128)} reshape(f32[512,16,16]{2,1,0:T(8,128)} %bitcast.125) | data formatting | bytes 1048576
  120.0 3.5 %all-to-all-start.2 = ((f32[4,1,32768]{2,1,0:T(1,128)}), f32[4,1,32768]{2,1,0:T(1,128)S(1)}, u32[]{:S(2)}, u32[]{:S(2)}) async-start(f32[4,1,32768]{2,1,0:T(1,128)} %reshape.239), calls=%async_computation.2 | async-start | bytes 1048576 | tf_op jit(solution)/shard_map/all_to_all | solution.py:83
  123.5 24.7 %gather_fusion.1 = f32[4096]{0:T(1024)S(1)} fusion(f32[31]{0:T(128)S(1)} %copy-done, s32[4096]{0:T(1024)S(1)} %broadcast_clamp_fusion.1), kind=kCustom, calls=%fused_computation.1.clone | custom fusion | bytes 49152 | tf_op jit(solution)/shard_map/jit(_take)/gather | solution.py:33
  150.5 3.4 %reshape.240 = f32[512,16,16]{2,1,0:T(8,128)} reshape(f32[4,32768]{1,0:T(4,128)S(1)} %reduce.1) | data formatting | bytes 1048576
  153.9 3.3 %copy.24 = f32[16,16,4,128]{3,0,2,1:T(8,128)S(1)} copy(f32[16,16,4,128]{1,0,3,2:T(8,128)} %bitcast.128) | data formatting | bytes 1048576 | tf_op jit(solution)/shard_map/all_to_all | solution.py:83
  158.0 15.2 %all_to_all.59 = f32[4,16,16,128]{3,1,2,0:T(8,128)S(1)} all-to-all(f32[4,16,16,128]{3,1,2,0:T(8,128)S(1)} %pad_maximum_fusion), channel_id=1, replica_groups=mesh['tile'=8,'slab'=4] {'slab'}, dimensions={0} | all-to-all | bytes 1048576 | tf_op jit(solution)/shard_map/all_to_all | solution.py:90
  173.8 22.9 %fusion.21 = f32[16,16,512]{2,1,0:T(8,128)S(1)} fusion(f32[16,16,512]{2,1,0:T(8,128)S(1)} %reshape.26, f32[]{:T(128)} %bitcast.35, f32[]{:T(128)} %bitcast.34, f32[]{:T(128)} %bitcast.33, f32[]{:T(128)} %bitcast.32, f32[]{:T(128)} %bitcast.31, f32[]{:T(128)} %bitcast.30, f32[]{:T(128)} %bitcast.29, f32[]{:T(128)} %bitcast.28, f32[]{:T(128)} %bitcast.27, ...), kind=kOutput, calls=%fused_computation.23 | convolution fusion | flops 824967168 | bytes 1048700 | tf_op jit(solution)/shard_map/dot_general | solution.py:59
  196.8 13.3 %collective-permute-start.2 = (f32[16,15,512]{2,1,0:T(8,128)S(1)}, f32[16,15,512]{2,1,0:T(8,128)S(1)}, u32[]{:S(2)}, u32[]{:S(2)}) collective-permute-start(f32[16,15,512]{2,1,0:T(8,128)S(1)} %get-tuple-element.4), channel_id=1, source_target_pairs={{0,4},{4,8},{8,12},{12,16},{16,20},{20,24},{24,28},{1,5},{5,9},{9,... | collective-permute-start | bytes 1474568 | tf_op jit(solution)/shard_map/ppermute | solution.py:16
  212.3 4.8 %gather_fusion = f32[736]{0:T(1024)S(1)} fusion(f32[31]{0:T(128)S(1)} %copy-done.1, s32[1024]{0:T(1024)S(1)} %pad_clamp_fusion.1), kind=kCustom, calls=%fused_computation.clone | custom fusion | bytes 8832 | tf_op jit(solution)/shard_map/jit(_take)/gather | solution.py:33
  217.2 3.4 %collective-permute-done.3 = f32[16,15,512]{2,1,0:T(8,128)S(1)} collective-permute-done((f32[16,15,512]{2,1,0:T(8,128)S(1)}, f32[16,15,512]{2,1,0:T(8,128)S(1)}, u32[]{:S(2)}, u32[]{:S(2)}) %collective-permute-start.3) | collective-permute-done | bytes 491552 | tf_op jit(solution)/shard_map/ppermute | solution.py:17
  (60 shorter events, 29.0 us)
Async XLA Ops:
  0.6 56.1 %copy-start = (f32[31]{0:T(128)S(1)}, f32[31]{0:T(128)}, u32[]{:S(2)}) copy-start(f32[31]{0:T(128)} %param.15) | copy-start | bytes 376
  0.6 7.9 %copy-start.1 = (f32[31]{0:T(128)S(1)}, f32[31]{0:T(128)}, u32[]{:S(2)}) copy-start(f32[31]{0:T(128)} %param.13) | copy-start | bytes 376
  2.0 12.9 %collective-permute-start = (f32[16,15,512]{2,1,0:T(8,128)S(1)}, f32[16,15,512]{2,1,0:T(8,128)S(1)}, u32[]{:S(2)}, u32[]{:S(2)}) collective-permute-start(f32[16,15,512]{2,1,0:T(8,128)S(1)} %get-tuple-element.11), channel_id=1, source_target_pairs={{0,4},{4,8},{8,12},{12,16},{16,20},{20,24},{24,28},{1,5},{5,9},{9,... | collective-permute-start | bytes 1474568 | tf_op jit(solution)/shard_map/ppermute | solution.py:16
  6.5 13.4 %collective-permute-start.1 = (f32[16,15,512]{2,1,0:T(8,128)S(1)}, f32[16,15,512]{2,1,0:T(8,128)S(1)}, u32[]{:S(2)}, u32[]{:S(2)}) collective-permute-start(f32[16,15,512]{2,1,0:T(8,128)S(1)} %get-tuple-element.12), channel_id=1, source_target_pairs={{4,0},{8,4},{12,8},{16,12},{20,16},{24,20},{28,24},{5,1},{9,5},{13... | collective-permute-start | bytes 1474568 | tf_op jit(solution)/shard_map/ppermute | solution.py:17
  8.6 4.9 %copy-start.5 = (f32[31]{0:T(128)S(1)}, f32[31]{0:T(128)}, u32[]{:S(2)}) copy-start(f32[31]{0:T(128)} %param.14) | copy-start | bytes 376
  8.6 11.3 %copy-start.2 = (f32[16,16,512]{2,1,0:T(8,128)S(1)}, f32[16,16,512]{2,1,0:T(8,128)}, u32[]{:S(2)}) copy-start(f32[16,16,512]{2,1,0:T(8,128)} %param.11) | copy-start | bytes 1572868
  52.1 29.5 %all-to-all-start = ((f32[4,1,32768]{2,1,0:T(1,128)}), f32[4,1,32768]{2,1,0:T(1,128)S(1)}, u32[]{:S(2)}, u32[]{:S(2)}) async-start(f32[4,1,32768]{2,1,0:T(1,128)} %reshape.237), calls=%async_computation | async-start | bytes 1048576 | tf_op jit(solution)/shard_map/all_to_all | solution.py:77
  91.0 6.3 %copy-start.3 = (f32[16,16,512]{2,1,0:T(8,128)S(1)}, f32[16,16,512]{2,1,0:T(8,128)}, u32[]{:S(2)}) copy-start(f32[16,16,512]{2,1,0:T(8,128)} %param.12) | copy-start | bytes 1572868
  92.8 13.7 %all-to-all-start.1 = ((f32[64,16,128]{2,1,0:T(8,128)}), f32[64,16,128]{2,1,0:T(8,128)S(1)}, u32[]{:S(2)}, u32[]{:S(2)}) async-start(f32[64,16,128]{2,1,0:T(8,128)} %copy.21), calls=%async_computation.1 | async-start | bytes 1048576 | tf_op jit(solution)/shard_map/all_to_all | solution.py:80
  120.0 28.4 %all-to-all-start.2 = ((f32[4,1,32768]{2,1,0:T(1,128)}), f32[4,1,32768]{2,1,0:T(1,128)S(1)}, u32[]{:S(2)}, u32[]{:S(2)}) async-start(f32[4,1,32768]{2,1,0:T(1,128)} %reshape.239), calls=%async_computation.2 | async-start | bytes 1048576 | tf_op jit(solution)/shard_map/all_to_all | solution.py:83
  196.8 20.4 %collective-permute-start.2 = (f32[16,15,512]{2,1,0:T(8,128)S(1)}, f32[16,15,512]{2,1,0:T(8,128)S(1)}, u32[]{:S(2)}, u32[]{:S(2)}) collective-permute-start(f32[16,15,512]{2,1,0:T(8,128)S(1)} %get-tuple-element.4), channel_id=1, source_target_pairs={{0,4},{4,8},{8,12},{12,16},{16,20},{20,24},{24,28},{1,5},{5,9},{9,... | collective-permute-start | bytes 1474568 | tf_op jit(solution)/shard_map/ppermute | solution.py:16
  210.1 10.5 %collective-permute-start.3 = (f32[16,15,512]{2,1,0:T(8,128)S(1)}, f32[16,15,512]{2,1,0:T(8,128)S(1)}, u32[]{:S(2)}, u32[]{:S(2)}) collective-permute-start(f32[16,15,512]{2,1,0:T(8,128)S(1)} %get-tuple-element.6), channel_id=1, source_target_pairs={{4,0},{8,4},{12,8},{16,12},{20,16},{24,20},{28,24},{5,1},{9,5},{13... | collective-permute-start | bytes 1474568 | tf_op jit(solution)/shard_map/ppermute | solution.py:17
  221.6 8.8 %copy-start.4 = (f32[16,16,512]{2,1,0:T(8,128)}, f32[16,16,512]{2,1,0:T(8,128)S(1)}, u32[]{:S(2)}) copy-start(f32[16,16,512]{2,1,0:T(8,128)S(1)} %fusion.18) | copy-start | bytes 1572868
  222.3 4.4 %collective-permute-start.4 = (f32[16,1,256]{2,1,0:T(1,128)S(1)}, f32[16,1,256]{2,1,0:T(1,128)S(1)}, u32[]{:S(2)}, u32[]{:S(2)}) collective-permute-start(f32[16,1,256]{2,1,0:T(1,128)S(1)} %get-tuple-element.13), channel_id=1, source_target_pairs={{0,4},{4,8},{8,12},{12,16},{16,20},{20,24},{24,28},{1,5},{5,9},{9,... | collective-permute-start | bytes 49160 | tf_op jit(solution)/shard_map/ppermute | solution.py:16
  224.3 5.1 %collective-permute-start.5 = (f32[16,1,256]{2,1,0:T(1,128)S(1)}, f32[16,1,256]{2,1,0:T(1,128)S(1)}, u32[]{:S(2)}, u32[]{:S(2)}) collective-permute-start(f32[16,1,256]{2,1,0:T(1,128)S(1)} %get-tuple-element.14), channel_id=1, source_target_pairs={{4,0},{8,4},{12,8},{16,12},{20,16},{24,20},{28,24},{5,1},{9,5},{13... | collective-permute-start | bytes 49160 | tf_op jit(solution)/shard_map/ppermute | solution.py:17
